TPU v7x, 512 devices: a whole 4x8x8 slice. The times are simulated.
512 devices in a mesh: dp: 32 (over y, z_lo, core), seq: 16 (over x, z_hi).
Axes of the slice: x: 4, y: 8, z: 8 (z_hi: 4, z_lo: 2; z = z_hi * 2 + z_lo), core: 2. Of those that a mesh axis runs over, the one named last changes fastest.
Arguments:
- query_rows: bfloat16 [32, 2048, 2048], P('dp', 'seq'), may hold values from -6 to 6
- key_rows: bfloat16 [32, 2048, 2048], P('dp', 'seq'), may hold values from -0.5 to 0.5
- value_rows: bfloat16 [32, 2048, 2048], P('dp', 'seq'), may hold values from -6 to 6
- doc_starts: int32 [32, 2048], P('dp', 'seq'), may hold values 0 or 1
- decay_rates: int32 [16], replicated, may hold values from 1 to 100
- out_gain: float32 [2048], replicated, may hold values from 0.1 to 1.9
- cotangent: bfloat16 [32, 2048, 2048], P('dp', 'seq'), may hold values from -6 to 6
Outputs:
- normed: bfloat16 [32, 2048, 2048], P('dp', 'seq')
- grad_query: bfloat16 [32, 2048, 2048], P('dp', 'seq')
- grad_key: bfloat16 [32, 2048, 2048], P('dp', 'seq')
- grad_value: bfloat16 [32, 2048, 2048], P('dp', 'seq')
- grad_gain: float32 [2048], P('dp')
All inputs are finite; a program needn't handle non-finite values. No bound on the sum of `doc_starts` on one device may be relied on, other than what follows from the above.
Results may differ from a plain program's by a relative error of at most 0.00085.
Values may be sent and summed in bfloat16 or wider, within the bound.
No kernel may reach another device: no remote copies, remote signals or barrier semaphores. Data moves between devices by JAX's collectives and lax.ppermute only.
A program may use at most 64 MiB of HBM per device.

v0:
```python
import math
import jax
import jax.numpy as jnp
from jax import lax
from jax.sharding import PartitionSpec as P

E = 128
highest = lax.Precision.HIGHEST
epsilon = 1e-05


def pack(factor, state):
    heads, width, _ = state.shape
    rows = jnp.broadcast_to(factor[:, None, None], (heads, 8, width))
    return jnp.concatenate([state, rows], axis=1)


def scan_exclusive(factor, state, reverse):
    count = lax.axis_size("seq")
    width = state.shape[1]
    run_factor, run_state = (factor, state)
    out_factor, out_state = (jnp.ones_like(factor), jnp.zeros_like(state))
    distance = 1
    while distance < count:
        if reverse:
            pairs = [(i, i - distance) for i in range(distance, count)]
        else:
            pairs = [(i, i + distance) for i in range(count - distance)]
        got = lax.ppermute(pack(run_factor, run_state), "seq", pairs)
        got_state, got_factor = (got[:, :width], got[:, width, 0])
        out_state = out_state + out_factor[:, None, None] * got_state
        out_factor = out_factor * got_factor
        if distance * 2 < count:
            run_state = run_state + run_factor[:, None, None] * got_state
            run_factor = run_factor * got_factor
        distance *= 2
    return out_state


def block_terms(log_decay, marks):
    length = marks.shape[0]
    counted = jnp.cumsum(marks, dtype=jnp.int32)
    places = jnp.arange(length, dtype=jnp.float32)
    offsets = places[:, None] - places[None, :]
    inside = (counted[:, None] == counted[None, :]) & (offsets >= 0.0)
    weights = jnp.where(
        inside[None], jnp.exp2(log_decay[:, None, None] * jnp.maximum(offsets, 0.0)[None]), 0.0
    )
    fresh = (counted == 0).astype(jnp.float32)
    entry = fresh[:, None] * jnp.exp2(log_decay[None, :] * (places[:, None] + 1.0))
    latest = counted[length - 1]
    tail = jnp.where(
        (counted == latest)[:, None],
        jnp.exp2(log_decay[None, :] * (length - 1.0 - places)[:, None]),
        0.0,
    )
    through = (latest == 0).astype(jnp.float32) * jnp.exp2(log_decay * length)
    return (weights, entry, tail, through)


def state_sum(key_block, value_block, tail):
    return jnp.einsum("jhe,jhf->hef", key_block * tail[:, :, None], value_block, precision=highest)


def out_sum(query_block, key_block, value_block, state_in, weights, entry):
    scores = jnp.einsum("ihe,jhe->hij", query_block, key_block, precision=highest) * weights
    inner = jnp.einsum("hij,jhe->ihe", scores, value_block, precision=highest)
    carried = jnp.einsum("ihe,hef->ihf", query_block, state_in, precision=highest)
    return inner + entry[:, :, None] * carried


def run_chain(through, terms, start, backward):

    def advance(accum, item):
        factor, term = item
        return (factor[:, None, None] * accum + term, accum)

    return lax.scan(advance, start, (through, terms), reverse=backward)


def ahead_state(factor, state):
    return scan_exclusive(factor, state, False)


def behind_grad(factor, state):
    return scan_exclusive(factor, state, True)


def forward_local(query_seq, key_seq, value_seq, marks, log_decay, link):
    length, heads, width = query_seq.shape
    block = math.gcd(length, 512)
    count = length // block
    query_blocks = query_seq.astype(jnp.float32).reshape(count, block, heads, width)
    key_blocks = key_seq.astype(jnp.float32).reshape(count, block, heads, width)
    value_blocks = value_seq.astype(jnp.float32).reshape(count, block, heads, width)
    weights, entry, tail, through = jax.vmap(block_terms, (None, 0))(
        log_decay, marks.reshape(count, block)
    )

    def states_of(key_part, value_part):
        return jax.vmap(state_sum)(key_part, value_part, tail)

    states, state_back = jax.vjp(states_of, key_blocks, value_blocks)
    empty = jnp.zeros((heads, width, width), jnp.float32)
    own_state = run_chain(through, states, empty, False)[0]
    own_factor = jnp.prod(through, axis=0)
    device_in = link(own_factor, own_state)
    block_in = run_chain(through, states, device_in, False)[1]

    def outs_of(query_part, key_part, value_part, state_part):
        return jax.vmap(out_sum)(query_part, key_part, value_part, state_part, weights, entry)

    outs, out_back = jax.vjp(outs_of, query_blocks, key_blocks, value_blocks, block_in)
    saved = (through, own_factor, state_back, out_back, block, count)
    return (outs.reshape(length, heads * width), saved)


def backward_local(grad_rows, saved, link, heads, width):
    through, own_factor, state_back, out_back, block, count = saved
    length = grad_rows.shape[0]
    grad_blocks = grad_rows.reshape(count, block, heads, width)
    grad_q_part, grad_k_part, grad_v_part, grad_state = out_back(grad_blocks)
    empty = jnp.zeros((heads, width, width), jnp.float32)
    own_grad = run_chain(through, grad_state, empty, True)[0]
    device_out = link(own_factor, own_grad)
    block_out = run_chain(through, grad_state, device_out, True)[1]
    extra_key, extra_value = state_back(block_out)
    flat = (length, heads * width)
    return (
        grad_q_part.reshape(flat),
        (grad_k_part + extra_key).reshape(flat),
        (grad_v_part + extra_value).reshape(flat),
    )


def normalize(mixed, out_gain, cotangent):

    def apply(attn, gain_vec):
        scale = lax.rsqrt(jnp.mean(attn * attn, axis=-1, keepdims=True) + epsilon)
        return attn * scale * gain_vec

    result, back = jax.vjp(apply, mixed, out_gain)
    grad_out, gain_part = back(cotangent.astype(jnp.float32))
    return (result.astype(jnp.bfloat16), grad_out, gain_part)


def per_device(query_rows, key_rows, value_rows, doc_starts, decay_rates, out_gain, cotangent):
    local_tokens = query_rows.shape[1]
    total = local_tokens * lax.axis_size("seq")
    log_decay = -decay_rates.astype(jnp.float32) / total
    heads = query_rows.shape[2] // E
    shaped = (local_tokens, heads, E)
    outs, saved = forward_local(
        query_rows[0].reshape(shaped),
        key_rows[0].reshape(shaped),
        value_rows[0].reshape(shaped),
        doc_starts[0],
        log_decay,
        ahead_state,
    )
    normed, grad_out, gain_part = normalize(outs[None], out_gain, cotangent)
    grads = backward_local(grad_out[0], saved, behind_grad, heads, E)
    grad_query = grads[0][None].astype(jnp.bfloat16)
    grad_key = grads[1][None].astype(jnp.bfloat16)
    grad_value = grads[2][None].astype(jnp.bfloat16)
    summed = lax.psum(gain_part, ("dp", "seq"))
    share = summed.shape[-1] // lax.axis_size("dp")
    grad_gain = lax.dynamic_slice_in_dim(summed, lax.axis_index("dp") * share, share)
    return (normed, grad_query, grad_key, grad_value, grad_gain)


def solution(mesh):
    return jax.shard_map(
        per_device,
        mesh=mesh,
        in_specs=(
            P("dp", "seq", None),
            P("dp", "seq", None),
            P("dp", "seq", None),
            P("dp", "seq"),
            P(),
            P(),
            P("dp", "seq", None),
        ),
        out_specs=(
            P("dp", "seq", None),
            P("dp", "seq", None),
            P("dp", "seq", None),
            P("dp", "seq", None),
            P("dp"),
        ),
        check_vma=False,
    )
```

profile of v0, /device:TPU:1, one launch (start us, length us, event | category | flops | bytes accessed | tf_op | source)
XLA Modules:
  0.0 497.9 jit_solution(8573685035798244976)
XLA Ops:
  0.7 1.0 reduce_window_sum.11
  1.7 0.6 slice.45
  2.9 0.7 compare_convert_fusion
  3.6 1.1 copy.65
  5.0 1.3 convolution_add_fusion.2
  6.4 1.1 pad_maximum_fusion.1
  7.5 6.7 %collective-permute-start = (f32[16,136,128]{2,1,0:T(8,128)}, f32[16,136,128]{2,1,0:T(8,128)S(1)}, u32[]{:S(2)}, u32[]{:S(2)}) collective-permute-start(f32[16,136,128]{2,1,0:T(8,128)} %pad_maximum_fusion.1), channel_id=1, source_target_pairs={{0,1},{1,2},{2,3},{3,4},{4,5},{5,6},{6,7},{7,8},{8,9},{9,10},{10,1... | collective-permute-start | bytes 3342344 | tf_op jit(solution)/shard_map/ppermute | solution.py:29
  14.3 22.9 %collective-permute-done = f32[16,136,128]{2,1,0:T(8,128)S(1)} collective-permute-done((f32[16,136,128]{2,1,0:T(8,128)}, f32[16,136,128]{2,1,0:T(8,128)S(1)}, u32[]{:S(2)}, u32[]{:S(2)}) %collective-permute-start) | collective-permute-done | bytes 1114144 | tf_op jit(solution)/shard_map/ppermute | solution.py:29
  37.7 35.3 %collective-permute-start.1 = (f32[16,136,128]{2,1,0:T(8,128)S(1)}, f32[16,136,128]{2,1,0:T(8,128)S(1)}, u32[]{:S(2)}, u32[]{:S(2)}) collective-permute-start(f32[16,136,128]{2,1,0:T(8,128)S(1)} %pad_maximum_fusion.2), channel_id=1, source_target_pairs={{0,2},{1,3},{2,4},{3,5},{4,6},{5,7},{6,8},{7,9},{8,10},{9,11},{10,... | collective-permute-start | bytes 3342344 | tf_op jit(solution)/shard_map/ppermute | solution.py:29
  73.0 29.5 %collective-permute-done.1 = f32[16,136,128]{2,1,0:T(8,128)S(1)} collective-permute-done((f32[16,136,128]{2,1,0:T(8,128)S(1)}, f32[16,136,128]{2,1,0:T(8,128)S(1)}, u32[]{:S(2)}, u32[]{:S(2)}) %collective-permute-start.1) | collective-permute-done | bytes 1114144 | tf_op jit(solution)/shard_map/ppermute | solution.py:29
  102.7 0.8 copy-done.11
  103.9 3.9 collective-permute-start.2
  107.8 12.4 %collective-permute-done.2 = f32[16,136,128]{2,1,0:T(8,128)S(1)} collective-permute-done((f32[16,136,128]{2,1,0:T(8,128)S(1)}, f32[16,136,128]{2,1,0:T(8,128)S(1)}, u32[]{:S(2)}, u32[]{:S(2)}) %collective-permute-start.2) | collective-permute-done | bytes 1114144 | tf_op jit(solution)/shard_map/ppermute | solution.py:29
  120.3 0.8 copy-done.13
  121.5 1.1 pad_maximum_fusion.4
  122.5 6.3 %collective-permute-start.3 = (f32[16,136,128]{2,1,0:T(8,128)}, f32[16,136,128]{2,1,0:T(8,128)}, u32[]{:S(2)}, u32[]{:S(2)}) collective-permute-start(f32[16,136,128]{2,1,0:T(8,128)} %pad_maximum_fusion.4), channel_id=1, source_target_pairs={{0,8},{1,9},{2,10},{3,11},{4,12},{5,13},{6,14},{7,15},{16,24},{17,... | collective-permute-start | bytes 3342344 | tf_op jit(solution)/shard_map/ppermute | solution.py:29
  129.9 1.2 convolution_bitcast_fusion.4
  131.1 20.1 %collective-permute-done.3 = f32[16,136,128]{2,1,0:T(8,128)} collective-permute-done((f32[16,136,128]{2,1,0:T(8,128)}, f32[16,136,128]{2,1,0:T(8,128)}, u32[]{:S(2)}, u32[]{:S(2)}) %collective-permute-start.3) | collective-permute-done | bytes 1114144 | tf_op jit(solution)/shard_map/ppermute | solution.py:29
  151.2 1.6 fusion.13
  152.8 2.0 multiply_reduce_fusion
  154.8 1.6 copy.45
  156.9 1.6 add_add_fusion
  158.6 1.5 copy.48
  160.1 1.2 fusion
  161.4 1.3 collective-permute-start.4
  162.7 80.2 %collective-permute-done.4 = f32[16,136,128]{2,1,0:T(8,128)S(1)} collective-permute-done((f32[16,136,128]{2,1,0:T(8,128)S(1)}, f32[16,136,128]{2,1,0:T(8,128)S(1)}, u32[]{:S(2)}, u32[]{:S(2)}) %collective-permute-start.4) | collective-permute-done | bytes 1114144 | tf_op jit(solution)/shard_map/ppermute | solution.py:29
  243.5 1.3 collective-permute-start.5
  244.8 74.5 %collective-permute-done.5 = f32[16,136,128]{2,1,0:T(8,128)S(1)} collective-permute-done((f32[16,136,128]{2,1,0:T(8,128)S(1)}, f32[16,136,128]{2,1,0:T(8,128)S(1)}, u32[]{:S(2)}, u32[]{:S(2)}) %collective-permute-start.5) | collective-permute-done | bytes 1114144 | tf_op jit(solution)/shard_map/ppermute | solution.py:29
  319.5 0.8 copy-done.9
  320.5 1.1 pad_maximum_fusion.6
  321.7 1.3 collective-permute-start.6
  322.9 43.6 %collective-permute-done.6 = f32[16,136,128]{2,1,0:T(8,128)} collective-permute-done((f32[16,136,128]{2,1,0:T(8,128)}, f32[16,136,128]{2,1,0:T(8,128)}, u32[]{:S(2)}, u32[]{:S(2)}) %collective-permute-start.6) | collective-permute-done | bytes 1114144 | tf_op jit(solution)/shard_map/ppermute | solution.py:29
  366.6 1.4 multiply_add_fusion
  368.0 1.0 multiply_reduce_fusion.2
  369.1 1.1 pad_maximum_fusion.7
  370.2 1.5 collective-permute-start.7
  371.7 1.2 convolution_multiply_fusion
  372.9 1.2 fusion.23
  374.1 2.0 fusion.5
  376.1 2.0 copy.57
  378.2 108.3 %psum.7 = f32[2048]{0:T(1024)S(1)} all-reduce(f32[2048]{0:T(1024)S(1)} %get-tuple-element.64), channel_id=1, replica_groups=mesh['dp'=32,'seq'=16] {'dp','seq'}, use_global_device_ids=true, to_apply=%region_4.5 | all-reduce | flops 2048 | bytes 16384 | tf_op jit(solution)/shard_map/psum | solution.py:166
  487.0 1.8 convolution_bitcast_fusion.2
  488.9 1.2 fusion.40
  490.4 1.9 fusion.12
  492.4 2.3 fusion.6
  494.7 1.2 fusion.7
  495.9 1.0 copy.58
  496.9 1.0 copy.59
  (72 shorter events, 5.4 us)
Async XLA Ops:
  0.6 4.1 copy-start.16
  0.6 4.2 copy-start.19
  7.5 29.7 %collective-permute-start = (f32[16,136,128]{2,1,0:T(8,128)}, f32[16,136,128]{2,1,0:T(8,128)S(1)}, u32[]{:S(2)}, u32[]{:S(2)}) collective-permute-start(f32[16,136,128]{2,1,0:T(8,128)} %pad_maximum_fusion.1), channel_id=1, source_target_pairs={{0,1},{1,2},{2,3},{3,4},{4,5},{5,6},{6,7},{7,8},{8,9},{9,10},{10,1... | collective-permute-start | bytes 3342344 | tf_op jit(solution)/shard_map/ppermute | solution.py:29
  37.1 65.6 %copy-start.7 = (f32[16,136,128]{2,1,0:T(8,128)}, f32[16,136,128]{2,1,0:T(8,128)S(1)}, u32[]{:S(2)}) copy-start(f32[16,136,128]{2,1,0:T(8,128)S(1)} %collective-permute-done) | copy-start | bytes 3342340
  37.7 64.8 %collective-permute-start.1 = (f32[16,136,128]{2,1,0:T(8,128)S(1)}, f32[16,136,128]{2,1,0:T(8,128)S(1)}, u32[]{:S(2)}, u32[]{:S(2)}) collective-permute-start(f32[16,136,128]{2,1,0:T(8,128)S(1)} %pad_maximum_fusion.2), channel_id=1, source_target_pairs={{0,2},{1,3},{2,4},{3,5},{4,6},{5,7},{6,8},{7,9},{8,10},{9,11},{10,... | collective-permute-start | bytes 3342344 | tf_op jit(solution)/shard_map/ppermute | solution.py:29
  102.5 1.0 copy-start.11
  103.9 16.3 %collective-permute-start.2 = (f32[16,136,128]{2,1,0:T(8,128)S(1)}, f32[16,136,128]{2,1,0:T(8,128)S(1)}, u32[]{:S(2)}, u32[]{:S(2)}) collective-permute-start(f32[16,136,128]{2,1,0:T(8,128)S(1)} %pad_maximum_fusion.3), channel_id=1, source_target_pairs={{0,4},{1,5},{2,6},{3,7},{4,8},{5,9},{6,10},{7,11},{8,12},{9,13},{1... | collective-permute-start | bytes 3342344 | tf_op jit(solution)/shard_map/ppermute | solution.py:29
  120.2 1.0 copy-start.13
  121.5 7.4 %copy-start.17 = (bf16[1,128,2048]{2,1,0:T(8,128)(2,1)S(1)}, bf16[1,128,2048]{2,1,0:T(8,128)(2,1)}, u32[]{:S(2)}) copy-start(bf16[1,128,2048]{2,1,0:T(8,128)(2,1)} %param.7) | copy-start | bytes 1572868
  122.5 28.6 %collective-permute-start.3 = (f32[16,136,128]{2,1,0:T(8,128)}, f32[16,136,128]{2,1,0:T(8,128)}, u32[]{:S(2)}, u32[]{:S(2)}) collective-permute-start(f32[16,136,128]{2,1,0:T(8,128)} %pad_maximum_fusion.4), channel_id=1, source_target_pairs={{0,8},{1,9},{2,10},{3,11},{4,12},{5,13},{6,14},{7,15},{16,24},{17,... | collective-permute-start | bytes 3342344 | tf_op jit(solution)/shard_map/ppermute | solution.py:29
  129.2 30.9 %copy-start.2 = (bf16[1,128,2048]{1,2,0:T(8,128)(2,1)}, bf16[1,128,2048]{1,2,0:T(8,128)(2,1)S(1)}, u32[]{:S(2)}) copy-start(bf16[1,128,2048]{1,2,0:T(8,128)(2,1)S(1)} %copy.64) | copy-start | bytes 1572868
  129.3 21.9 %copy-start.14 = (f32[16,136,128]{2,1,0:T(8,128)S(1)}, f32[16,136,128]{2,1,0:T(8,128)}, u32[]{:S(2)}) copy-start(f32[16,136,128]{2,1,0:T(8,128)} %copy-done.13) | copy-start | bytes 3342340
  129.8 1.2 copy-start.3
  129.9 21.3 %copy-start.8 = (f32[16,136,128]{2,1,0:T(8,128)S(1)}, f32[16,136,128]{2,1,0:T(8,128)}, u32[]{:S(2)}) copy-start(f32[16,136,128]{2,1,0:T(8,128)} %copy-done.7) | copy-start | bytes 3342340
  129.9 21.3 %copy-start.12 = (f32[16,136,128]{2,1,0:T(8,128)S(1)}, f32[16,136,128]{2,1,0:T(8,128)}, u32[]{:S(2)}) copy-start(f32[16,136,128]{2,1,0:T(8,128)} %copy-done.11) | copy-start | bytes 3342340
  152.8 2.0 copy-start
  154.8 1.6 copy-start.15
  154.8 1.6 copy-start.18
  161.4 81.5 %collective-permute-start.4 = (f32[16,136,128]{2,1,0:T(8,128)S(1)}, f32[16,136,128]{2,1,0:T(8,128)S(1)}, u32[]{:S(2)}, u32[]{:S(2)}) collective-permute-start(f32[16,136,128]{2,1,0:T(8,128)S(1)} %pad_maximum_fusion), channel_id=1, source_target_pairs={{1,0},{2,1},{3,2},{4,3},{5,4},{6,5},{7,6},{8,7},{9,8},{10,9},{11,1... | collective-permute-start | bytes 3342344 | tf_op jit(solution)/shard_map/ppermute | solution.py:29
  242.9 76.5 %copy-start.5 = (f32[16,136,128]{2,1,0:T(8,128)}, f32[16,136,128]{2,1,0:T(8,128)S(1)}, u32[]{:S(2)}) copy-start(f32[16,136,128]{2,1,0:T(8,128)S(1)} %collective-permute-done.4) | copy-start | bytes 3342340
  243.5 75.8 %collective-permute-start.5 = (f32[16,136,128]{2,1,0:T(8,128)S(1)}, f32[16,136,128]{2,1,0:T(8,128)S(1)}, u32[]{:S(2)}, u32[]{:S(2)}) collective-permute-start(f32[16,136,128]{2,1,0:T(8,128)S(1)} %pad_maximum_fusion.5), channel_id=1, source_target_pairs={{2,0},{3,1},{4,2},{5,3},{6,4},{7,5},{8,6},{9,7},{10,8},{11,9},{12,... | collective-permute-start | bytes 3342344 | tf_op jit(solution)/shard_map/ppermute | solution.py:29
  319.3 1.0 copy-start.9
  321.7 44.9 %collective-permute-start.6 = (f32[16,136,128]{2,1,0:T(8,128)}, f32[16,136,128]{2,1,0:T(8,128)}, u32[]{:S(2)}, u32[]{:S(2)}) collective-permute-start(f32[16,136,128]{2,1,0:T(8,128)} %pad_maximum_fusion.6), channel_id=1, source_target_pairs={{4,0},{5,1},{6,2},{7,3},{8,4},{9,5},{10,6},{11,7},{12,8},{13,9},{1... | collective-permute-start | bytes 3342344 | tf_op jit(solution)/shard_map/ppermute | solution.py:29
  370.2 119.8 %collective-permute-start.7 = (f32[16,136,128]{2,1,0:T(8,128)}, f32[16,136,128]{2,1,0:T(8,128)}, u32[]{:S(2)}, u32[]{:S(2)}) collective-permute-start(f32[16,136,128]{2,1,0:T(8,128)} %pad_maximum_fusion.7), channel_id=1, source_target_pairs={{8,0},{9,1},{10,2},{11,3},{12,4},{13,5},{14,6},{15,7},{24,16},{25,... | collective-permute-start | bytes 3342344 | tf_op jit(solution)/shard_map/ppermute | solution.py:29
  372.9 1.2 copy-start.1
  487.0 1.8 copy-start.4
  488.8 1.2 copy-start.6
  488.9 1.6 copy-start.10
where the time goes:
time: 499 us; the launch traced here: 498 us
  waiting for transfers between devices  283 us (57%)
  blocking collectives  108 us (22%)
  starting transfers between devices  57.6 us (12%)
  matrix products  17.2 us (3%)
  other arithmetic  16.4 us (3%)
  local copies, waits for them, and re-layouts  13.5 us (3%)
    ppermute x8, waiting for transfers between devices, scan_exclusive(): got = lax.ppermute(pack(run_factor, run_state), 'seq', pairs)  283 us
    psum x1, blocking collectives, per_device(): summed = lax.psum(gain_part, ('dp', 'seq'))  108 us
    ppermute x8, starting transfers between devices, scan_exclusive(): got = lax.ppermute(pack(run_factor, run_state), 'seq', pairs)  57.6 us
  transfers between devices with their start and end apart: 8, of which 7 were waited for; matrix products, arithmetic and copies ran while one was open for 2% of the time, Pallas kernels for 0%

commit v1 on v0

--- a/solution.py
+++ b/solution.py
@@ -163,7 +163,7 @@
     grad_query = grads[0][None].astype(jnp.bfloat16)
     grad_key = grads[1][None].astype(jnp.bfloat16)
     grad_value = grads[2][None].astype(jnp.bfloat16)
-    summed = lax.psum(gain_part, ("dp", "seq"))
+    summed = lax.all_gather(gain_part, ("dp", "seq")).sum(axis=0)
     share = summed.shape[-1] // lax.axis_size("dp")
     grad_gain = lax.dynamic_slice_in_dim(summed, lax.axis_index("dp") * share, share)
     return (normed, grad_query, grad_key, grad_value, grad_gain)

time: 499 us -> 1670 us (3.35)
  waiting for transfers between devices: 283 us -> 1530 us
  blocking collectives: 108 us -> 0 us
    all_gather x0 -> x1, waiting for transfers between devices: none -> 1220 us  [per_device(): summed = lax.all_gather(gain_part, ('dp', 'seq')).sum(axis=0)]
    psum x1 -> x0, blocking collectives: 108 us -> none  [per_device(): summed = lax.psum(gain_part, ('dp', 'seq'))]
    ppermute x8, waiting for transfers between devices: 283 us -> 306 us  [scan_exclusive(): got = lax.ppermute(pack(run_factor, run_state), 'seq', pairs)]
  transfers between devices with their start and end apart: 8 -> 9, of which waited for: 7 -> 9; matrix products, arithmetic and copies ran while one was open for 2% -> 2% of each run, Pallas kernels for 0% -> 0%
where the time goes in v1:
time: 1670 us; the launch traced here: 1660 us
  waiting for transfers between devices  1530 us (92%)
  starting transfers between devices  57.6 us (3%)
  other arithmetic  19.5 us (1%)
  local copies, waits for them, and re-layouts  18.6 us (1%)
  matrix products  18 us (1%)
    all_gather x1, waiting for transfers between devices, per_device(): summed = lax.all_gather(gain_part, ('dp', 'seq')).sum(axis=0)  1220 us
    ppermute x8, waiting for transfers between devices, scan_exclusive(): got = lax.ppermute(pack(run_factor, run_state), 'seq', pairs)  306 us
    ppermute x8, starting transfers between devices, scan_exclusive(): got = lax.ppermute(pack(run_factor, run_state), 'seq', pairs)  57.5 us
  transfers between devices with their start and end apart: 9, of which 9 were waited for; matrix products, arithmetic and copies ran while one was open for 2% of the time, Pallas kernels for 0%

profile of v1, /device:TPU:1, one launch (start us, length us, event | category | flops | bytes accessed | tf_op | source)
XLA Modules:
  0.0 1658.9 jit_solution(12745137814062521020)
XLA Ops:
  7.2 1.0 reduce_window_sum.11
  9.5 1.1 copy.113
  11.5 1.3 convolution_add_fusion.2
  13.0 1.1 pad_maximum_fusion.1
  14.0 6.7 collective-permute-start
  20.8 22.9 %collective-permute-done = f32[16,136,128]{2,1,0:T(8,128)S(1)} collective-permute-done((f32[16,136,128]{2,1,0:T(8,128)}, f32[16,136,128]{2,1,0:T(8,128)S(1)}, u32[]{:S(2)}, u32[]{:S(2)}) %collective-permute-start) | collective-permute-done | bytes 1114144 | tf_op jit(solution)/shard_map/ppermute | solution.py:29
  44.2 35.3 %collective-permute-start.1 = (f32[16,136,128]{2,1,0:T(8,128)S(1)}, f32[16,136,128]{2,1,0:T(8,128)S(1)}, u32[]{:S(2)}, u32[]{:S(2)}) collective-permute-start(f32[16,136,128]{2,1,0:T(8,128)S(1)} %pad_maximum_fusion.2), channel_id=1, source_target_pairs={{0,2},{1,3},{2,4},{3,5},{4,6},{5,7},{6,8},{7,9},{8,10},{9,11},{10,... | collective-permute-start | bytes 3342344 | tf_op jit(solution)/shard_map/ppermute | solution.py:29
  79.6 29.5 %collective-permute-done.1 = f32[16,136,128]{2,1,0:T(8,128)S(1)} collective-permute-done((f32[16,136,128]{2,1,0:T(8,128)S(1)}, f32[16,136,128]{2,1,0:T(8,128)S(1)}, u32[]{:S(2)}, u32[]{:S(2)}) %collective-permute-start.1) | collective-permute-done | bytes 1114144 | tf_op jit(solution)/shard_map/ppermute | solution.py:29
  110.3 3.9 collective-permute-start.2
  114.2 12.4 collective-permute-done.2
  126.7 0.8 copy-done.13
  127.9 1.1 pad_maximum_fusion.4
  128.9 6.3 collective-permute-start.3
  136.2 1.2 convolution_bitcast_fusion.4
  137.4 20.1 %collective-permute-done.3 = f32[16,136,128]{2,1,0:T(8,128)} collective-permute-done((f32[16,136,128]{2,1,0:T(8,128)}, f32[16,136,128]{2,1,0:T(8,128)}, u32[]{:S(2)}, u32[]{:S(2)}) %collective-permute-start.3) | collective-permute-done | bytes 1114144 | tf_op jit(solution)/shard_map/ppermute | solution.py:29
  157.6 1.6 fusion.13
  159.2 2.0 multiply_reduce_fusion
  161.2 1.6 copy.93
  162.9 1.0 fusion.11
  163.9 1.6 add_add_fusion
  165.5 1.5 copy.96
  167.1 1.2 fusion
  168.4 1.3 collective-permute-start.4
  169.7 80.6 %collective-permute-done.4 = f32[16,136,128]{2,1,0:T(8,128)S(1)} collective-permute-done((f32[16,136,128]{2,1,0:T(8,128)S(1)}, f32[16,136,128]{2,1,0:T(8,128)S(1)}, u32[]{:S(2)}, u32[]{:S(2)}) %collective-permute-start.4) | collective-permute-done | bytes 1114144 | tf_op jit(solution)/shard_map/ppermute | solution.py:29
  250.8 1.3 collective-permute-start.5
  252.1 75.0 %collective-permute-done.5 = f32[16,136,128]{2,1,0:T(8,128)S(1)} collective-permute-done((f32[16,136,128]{2,1,0:T(8,128)S(1)}, f32[16,136,128]{2,1,0:T(8,128)S(1)}, u32[]{:S(2)}, u32[]{:S(2)}) %collective-permute-start.5) | collective-permute-done | bytes 1114144 | tf_op jit(solution)/shard_map/ppermute | solution.py:29
  328.2 1.1 pad_maximum_fusion.6
  329.3 1.3 collective-permute-start.6
  330.6 43.3 %collective-permute-done.6 = f32[16,136,128]{2,1,0:T(8,128)} collective-permute-done((f32[16,136,128]{2,1,0:T(8,128)}, f32[16,136,128]{2,1,0:T(8,128)}, u32[]{:S(2)}, u32[]{:S(2)}) %collective-permute-start.6) | collective-permute-done | bytes 1114144 | tf_op jit(solution)/shard_map/ppermute | solution.py:29
  373.9 1.0 multiply_reduce_fusion.2
  374.9 1.4 multiply_add_fusion
  376.4 1.2 pad_maximum_fusion.7
  377.6 1.5 collective-permute-start.7
  379.0 1.2 convolution_multiply_fusion
  380.3 1.2 fusion.23
  381.5 2.0 fusion.5
  383.5 2.0 copy.105
  385.5 1.8 convolution_bitcast_fusion.2
  387.4 1.1 fusion.40
  388.5 21.9 %collective-permute-done.7 = f32[16,136,128]{2,1,0:T(8,128)} collective-permute-done((f32[16,136,128]{2,1,0:T(8,128)}, f32[16,136,128]{2,1,0:T(8,128)}, u32[]{:S(2)}, u32[]{:S(2)}) %collective-permute-start.7) | collective-permute-done | bytes 1114144 | tf_op jit(solution)/shard_map/ppermute | solution.py:29
  410.4 1.9 fusion.12
  412.3 2.0 fusion.7
  414.4 2.0 copy.106
  416.4 2.3 fusion.6
  418.7 1.0 copy.107
  419.7 1224.4 %all-gather.3.cloned.1.call-done = f32[1048576]{0:T(1024)} async-done(((f32[2048]{0:T(1024)}), f32[1048576]{0:T(1024)}) %all-gather.3.cloned.1.call-update) | async-done | bytes 4194320 | tf_op jit(solution)/shard_map/all_gather | solution.py:166
  1644.1 4.9 reshape.553
  1649.0 2.4 reduce_sum.41
  (76 shorter events, 7.1 us)
Async XLA Ops:
  7.2 3.5 copy-start.16
  7.2 4.3 copy-start.19
  7.2 1636.9 %all-gather.3.cloned.1.call-start = ((), (), s32[]{:S(2)}) async-start(), calls=%async_computation | async-start | bytes 4202496 | tf_op jit(solution)/shard_map/all_gather | solution.py:166
  14.0 29.7 %collective-permute-start = (f32[16,136,128]{2,1,0:T(8,128)}, f32[16,136,128]{2,1,0:T(8,128)S(1)}, u32[]{:S(2)}, u32[]{:S(2)}) collective-permute-start(f32[16,136,128]{2,1,0:T(8,128)} %pad_maximum_fusion.1), channel_id=1, source_target_pairs={{0,1},{1,2},{2,3},{3,4},{4,5},{5,6},{6,7},{7,8},{8,9},{9,10},{10,1... | collective-permute-start | bytes 3342344 | tf_op jit(solution)/shard_map/ppermute | solution.py:29
  43.7 65.4 %copy-start.7 = (f32[16,136,128]{2,1,0:T(8,128)}, f32[16,136,128]{2,1,0:T(8,128)S(1)}, u32[]{:S(2)}) copy-start(f32[16,136,128]{2,1,0:T(8,128)S(1)} %collective-permute-done) | copy-start | bytes 3342340
  44.2 64.9 %collective-permute-start.1 = (f32[16,136,128]{2,1,0:T(8,128)S(1)}, f32[16,136,128]{2,1,0:T(8,128)S(1)}, u32[]{:S(2)}, u32[]{:S(2)}) collective-permute-start(f32[16,136,128]{2,1,0:T(8,128)S(1)} %pad_maximum_fusion.2), channel_id=1, source_target_pairs={{0,2},{1,3},{2,4},{3,5},{4,6},{5,7},{6,8},{7,9},{8,10},{9,11},{10,... | collective-permute-start | bytes 3342344 | tf_op jit(solution)/shard_map/ppermute | solution.py:29
  109.1 1.0 copy-start.11
  110.3 16.3 collective-permute-start.2
  126.5 1.0 copy-start.13
  127.8 7.4 copy-start.17
  128.9 28.6 %collective-permute-start.3 = (f32[16,136,128]{2,1,0:T(8,128)}, f32[16,136,128]{2,1,0:T(8,128)}, u32[]{:S(2)}, u32[]{:S(2)}) collective-permute-start(f32[16,136,128]{2,1,0:T(8,128)} %pad_maximum_fusion.4), channel_id=1, source_target_pairs={{0,8},{1,9},{2,10},{3,11},{4,12},{5,13},{6,14},{7,15},{16,24},{17,... | collective-permute-start | bytes 3342344 | tf_op jit(solution)/shard_map/ppermute | solution.py:29
  135.5 31.6 %copy-start.2 = (bf16[1,128,2048]{1,2,0:T(8,128)(2,1)}, bf16[1,128,2048]{1,2,0:T(8,128)(2,1)S(1)}, u32[]{:S(2)}) copy-start(bf16[1,128,2048]{1,2,0:T(8,128)(2,1)S(1)} %copy.112) | copy-start | bytes 1572868
  135.6 21.9 %copy-start.14 = (f32[16,136,128]{2,1,0:T(8,128)S(1)}, f32[16,136,128]{2,1,0:T(8,128)}, u32[]{:S(2)}) copy-start(f32[16,136,128]{2,1,0:T(8,128)} %copy-done.13) | copy-start | bytes 3342340
  136.2 1.2 copy-start.3
  136.2 21.4 %copy-start.8 = (f32[16,136,128]{2,1,0:T(8,128)S(1)}, f32[16,136,128]{2,1,0:T(8,128)}, u32[]{:S(2)}) copy-start(f32[16,136,128]{2,1,0:T(8,128)} %copy-done.7) | copy-start | bytes 3342340
  136.2 21.4 %copy-start.12 = (f32[16,136,128]{2,1,0:T(8,128)S(1)}, f32[16,136,128]{2,1,0:T(8,128)}, u32[]{:S(2)}) copy-start(f32[16,136,128]{2,1,0:T(8,128)} %copy-done.11) | copy-start | bytes 3342340
  159.2 2.1 copy-start
  161.2 1.6 copy-start.15
  161.2 1.6 copy-start.18
  168.4 81.9 %collective-permute-start.4 = (f32[16,136,128]{2,1,0:T(8,128)S(1)}, f32[16,136,128]{2,1,0:T(8,128)S(1)}, u32[]{:S(2)}, u32[]{:S(2)}) collective-permute-start(f32[16,136,128]{2,1,0:T(8,128)S(1)} %pad_maximum_fusion), channel_id=1, source_target_pairs={{1,0},{2,1},{3,2},{4,3},{5,4},{6,5},{7,6},{8,7},{9,8},{10,9},{11,1... | collective-permute-start | bytes 3342344 | tf_op jit(solution)/shard_map/ppermute | solution.py:29
  250.3 76.8 %copy-start.5 = (f32[16,136,128]{2,1,0:T(8,128)}, f32[16,136,128]{2,1,0:T(8,128)S(1)}, u32[]{:S(2)}) copy-start(f32[16,136,128]{2,1,0:T(8,128)S(1)} %collective-permute-done.4) | copy-start | bytes 3342340
  250.8 76.3 %collective-permute-start.5 = (f32[16,136,128]{2,1,0:T(8,128)S(1)}, f32[16,136,128]{2,1,0:T(8,128)S(1)}, u32[]{:S(2)}, u32[]{:S(2)}) collective-permute-start(f32[16,136,128]{2,1,0:T(8,128)S(1)} %pad_maximum_fusion.5), channel_id=1, source_target_pairs={{2,0},{3,1},{4,2},{5,3},{6,4},{7,5},{8,6},{9,7},{10,8},{11,9},{12,... | collective-permute-start | bytes 3342344 | tf_op jit(solution)/shard_map/ppermute | solution.py:29
  327.1 1.0 copy-start.9
  329.3 44.6 %collective-permute-start.6 = (f32[16,136,128]{2,1,0:T(8,128)}, f32[16,136,128]{2,1,0:T(8,128)}, u32[]{:S(2)}, u32[]{:S(2)}) collective-permute-start(f32[16,136,128]{2,1,0:T(8,128)} %pad_maximum_fusion.6), channel_id=1, source_target_pairs={{4,0},{5,1},{6,2},{7,3},{8,4},{9,5},{10,6},{11,7},{12,8},{13,9},{1... | collective-permute-start | bytes 3342344 | tf_op jit(solution)/shard_map/ppermute | solution.py:29
  377.6 32.8 %collective-permute-start.7 = (f32[16,136,128]{2,1,0:T(8,128)}, f32[16,136,128]{2,1,0:T(8,128)}, u32[]{:S(2)}, u32[]{:S(2)}) collective-permute-start(f32[16,136,128]{2,1,0:T(8,128)} %pad_maximum_fusion.7), channel_id=1, source_target_pairs={{8,0},{9,1},{10,2},{11,3},{12,4},{13,5},{14,6},{15,7},{24,16},{25,... | collective-permute-start | bytes 3342344 | tf_op jit(solution)/shard_map/ppermute | solution.py:29
  380.2 1.2 copy-start.1
  385.5 1.8 copy-start.4
  387.3 23.1 %copy-start.6 = (f32[16,136,128]{2,1,0:T(8,128)S(1)}, f32[16,136,128]{2,1,0:T(8,128)}, u32[]{:S(2)}) copy-start(f32[16,136,128]{2,1,0:T(8,128)} %copy-done.5) | copy-start | bytes 3342340
  387.4 23.0 %copy-start.10 = (f32[16,136,128]{2,1,0:T(8,128)S(1)}, f32[16,136,128]{2,1,0:T(8,128)}, u32[]{:S(2)}) copy-start(f32[16,136,128]{2,1,0:T(8,128)} %copy-done.9) | copy-start | bytes 3342340
Sparse Core Ops, SparseCore 0:
  164.0 1480.0 all-gather.2
